TPU v7x, 32 devices: a whole 2x2x4 slice. The times are simulated.
32 devices in a mesh: tok: 4 (over y, x), ka: 4 (over z), out: 2 (over core).
Axes of the slice: x: 2, y: 2, z: 4, core: 2. Of those that a mesh axis runs over, the one named last changes fastest.
Arguments:
- features: bfloat16 [1024, 12288], P('tok', ('ka', 'out')), may hold values from -12 to 12, as said below
- lengths: int32 [4], P('tok'), may hold values from 1 to 256, 768 in all
- w_qkv: bfloat16 [12288, 24576], P(('ka', 'tok'), 'out'), may hold values from -0.0546875 to 0.0546875
- b_qkv: bfloat16 [24576], P(('out', 'ka')), may hold values from -2 to 2
- w_out: bfloat16 [8192, 12288], P(('out', 'tok'), 'ka'), may hold values from -0.0625 to 0.0625
- b_out: bfloat16 [12288], P(('ka', 'out')), may hold values from -3 to 3
Outputs:
- result: float32 [1024, 12288], P('tok', ('ka', 'out'))
Inputs may be any that keep to these rules, and one draw needn't show every extreme that they name: features: activations of order one; rows may differ in scale. `lengths`: live tokens of each prompt; some prompt is full.
All inputs are finite; a program needn't handle non-finite values. No bound on the sum of `lengths` on one device may be relied on, other than what follows from the above.
Results may differ from a plain program's by a relative error of at most 0.008.
Values may be sent and summed in bfloat16 or wider, within the bound.
No kernel may reach another device: no remote copies, remote signals or barrier semaphores. Data moves between devices by JAX's collectives and lax.ppermute only.
A program may use at most 192 MiB of HBM per device.

v0:
```python
import jax
import jax.numpy as jnp
from jax import lax
from jax.sharding import PartitionSpec as P

HD = 128
SEQ = 256


def softmax_rows(scores, allowed):
    scores = jnp.where(allowed, scores, -1e30)
    row_max = jnp.max(scores, axis=-1, keepdims=True)
    weights = jnp.exp(scores - row_max)
    row_sum = jnp.sum(weights, axis=-1, keepdims=True)
    return (weights / row_sum).astype(jnp.bfloat16)


def shards(features, lengths, w_qkv, b_qkv, w_out, b_out):
    row_count = features.shape[0]
    prompts = row_count // SEQ
    score_scale = 1.0 / HD**0.5
    panel = lax.all_gather(features, "out", axis=1, tiled=True)
    w_block = lax.all_gather(w_qkv, "tok", axis=0, tiled=True)
    partial_value = jnp.dot(panel, w_block, preferred_element_type=jnp.float32)
    qkv_sum = lax.psum_scatter(
        partial_value.astype(jnp.bfloat16), "ka", scatter_dimension=1, tiled=True
    ).astype(jnp.float32)
    qkv_held = (qkv_sum + b_qkv.astype(jnp.float32)).astype(jnp.bfloat16)
    heads_dev = qkv_held.shape[1] // (3 * HD)
    table = qkv_held.reshape(prompts, SEQ, heads_dev, 3, HD)
    positions = jnp.arange(SEQ)
    causal = positions[None, :] <= positions[:, None]
    live = positions[None, :] < lengths[:, None]
    allowed = causal[None, None] & live[:, None, None, :]
    scores = (
        jnp.einsum(
            "pshd,pthd->phst",
            table[:, :, :, 0],
            table[:, :, :, 1],
            preferred_element_type=jnp.float32,
        )
        * score_scale
    )
    prob_rows = softmax_rows(scores, allowed)
    context = jnp.einsum(
        "phst,pthd->pshd", prob_rows, table[:, :, :, 2], preferred_element_type=jnp.float32
    )
    context = context.astype(jnp.bfloat16).reshape(row_count, heads_dev * HD)
    head_group = lax.all_gather(context, "ka", axis=1, tiled=True)
    terms = jnp.dot(
        head_group,
        lax.all_gather(w_out, "tok", axis=0, tiled=True),
        preferred_element_type=jnp.float32,
    )
    summed = lax.psum_scatter(terms, "out", scatter_dimension=1, tiled=True)
    return summed + b_out.astype(jnp.float32)


def solution(mesh):
    placed = (
        P("tok", ("ka", "out")),
        P("tok"),
        P(("ka", "tok"), "out"),
        P(("out", "ka")),
        P(("out", "tok"), "ka"),
        P(("ka", "out")),
    )
    return jax.shard_map(
        shards, mesh=mesh, in_specs=placed, out_specs=P("tok", ("ka", "out")), check_vma=False
    )
```

profile of v0, /device:TPU:0, one launch (start us, length us, event | category | flops | bytes accessed | tf_op | source)
XLA Modules:
  0.0 1123.8 jit_solution(12351789201548837394)
XLA Ops:
  6.5 0.0 all-gather.5.cloned.1.call-start
  6.5 0.7 all-gather.5.cloned.1.call-update
  7.3 0.0 all-gather.7.cloned.1.call-start
  7.3 0.7 all-gather.7.cloned.1.call-update
  8.0 0.0 reduce-scatter.3.cloned.1.call-start
  8.1 13.4 %all-gather.5.cloned.1.call-done = bf16[256,3072]{1,0:T(8,128)(2,1)} async-done(((bf16[256,1536]{1,0:T(8,128)(2,1)}), bf16[256,3072]{1,0:T(8,128)(2,1)}) %all-gather.5.cloned.1.call-update) | async-done | bytes 1572880 | tf_op jit(solution)/shard_map/all_gather | solution.py:22
  21.4 650.2 %all-gather.7.cloned.1.call-done = bf16[3072,12288]{1,0:T(8,128)(2,1)} async-done(((bf16[768,12288]{1,0:T(8,128)(2,1)}), bf16[3072,12288]{1,0:T(8,128)(2,1)}) %all-gather.7.cloned.1.call-update) | async-done | bytes 75497488 | tf_op jit(solution)/shard_map/all_gather | solution.py:23
  671.6 31.1 %convolution_convert_fusion = bf16[256,12288]{1,0:T(8,128)(2,1)} fusion(bf16[256,3072]{1,0:T(8,128)(2,1)} %all-gather.5.cloned.1.call-done, bf16[3072,12288]{1,0:T(8,128)(2,1)} %all-gather.7.cloned.1.call-done), kind=kOutput, calls=%fused_computation.1 | convolution fusion | flops 19330498560 | bytes 83361792 | tf_op jit(solution)/shard_map/dot_general | solution.py:24
  702.7 0.0 reduce-scatter.3.cloned.1.call-update
  702.8 0.0 copy-start
  702.8 0.0 all-gather.11.cloned.1.call-start
  702.8 0.5 all-gather.11.cloned.1.call-update
  703.4 0.0 all-gather.9.cloned.1.call-start
  703.4 0.1 copy-done
  704.1 0.1 fusion.6
  704.2 109.4 %reduce-scatter.3.cloned.1.call-done = bf16[256,3072]{1,0:T(8,128)(2,1)} async-done(((bf16[256,12288]{1,0:T(8,128)(2,1)}), bf16[256,3072]{1,0:T(8,128)(2,1)}) %reduce-scatter.3.cloned.1.call-update) | async-done | bytes 1572880 | tf_op jit(solution)/shard_map/reduce_scatter | solution.py:25
  813.7 1.7 add_convert_fusion
  815.4 0.7 copy.11
  816.1 0.9 fusion.14
  817.0 2.0 convolution_convert_fusion.1
  819.0 0.0 all-gather.9.cloned.1.call-update
  819.0 0.0 reduce-scatter.5.cloned.1.call-start
  819.0 224.6 %all-gather.11.cloned.1.call-done = bf16[4096,3072]{1,0:T(8,128)(2,1)} async-done(((bf16[1024,3072]{1,0:T(8,128)(2,1)}), bf16[4096,3072]{1,0:T(8,128)(2,1)}) %all-gather.11.cloned.1.call-update) | async-done | bytes 25165840 | tf_op jit(solution)/shard_map/all_gather | solution.py:52
  1043.7 47.4 %all-gather.9.cloned.1.call-done = bf16[256,4096]{0,1:T(8,128)(2,1)} async-done(((bf16[256,1024]{0,1:T(8,128)(2,1)}), bf16[256,4096]{0,1:T(8,128)(2,1)}) %all-gather.9.cloned.1.call-update) | async-done | bytes 2097168 | tf_op jit(solution)/shard_map/all_gather | solution.py:49
  1091.1 13.3 %fusion.15 = f32[256,3072]{1,0:T(8,128)} fusion(bf16[256,4096]{0,1:T(8,128)(2,1)} %all-gather.9.cloned.1.call-done, bf16[4096,3072]{1,0:T(8,128)(2,1)} %all-gather.11.cloned.1.call-done), kind=kOutput, calls=%fused_computation.25 | convolution fusion | flops 6442450944 | bytes 30408704 | tf_op jit(solution)/shard_map/dot_general | solution.py:50
  1104.4 0.0 copy-start.1
  1104.4 0.0 reduce-scatter.5.cloned.1.call-update
  1104.4 0.7 copy-done.1
  1105.1 9.1 reduce-scatter.5.cloned.1.call-done
  1114.2 2.7 broadcast_add_fusion
  (3 shorter events, 0.0 us)
Async XLA Ops:
  6.5 14.9 %all-gather.5.cloned.1.call-start = ((), (), s32[]{:S(2)}) async-start(), calls=%async_computation.2 | async-start | bytes 2359296 | tf_op jit(solution)/shard_map/all_gather | solution.py:22
  7.3 664.4 %all-gather.7.cloned.1.call-start = ((), (), s32[]{:S(2)}) async-start(), calls=%async_computation.3 | async-start | bytes 94371840 | tf_op jit(solution)/shard_map/all_gather | solution.py:23
  8.0 805.7 %reduce-scatter.3.cloned.1.call-start = ((), (), s32[]{:S(2)}) async-start(), calls=%async_computation.4 | async-start | bytes 7864320 | tf_op jit(solution)/shard_map/reduce_scatter | solution.py:25
  702.8 0.7 copy-start
  702.8 340.9 %all-gather.11.cloned.1.call-start = ((), (), s32[]{:S(2)}) async-start(), calls=%async_computation.6 | async-start | bytes 31457280 | tf_op jit(solution)/shard_map/all_gather | solution.py:52
  703.4 387.7 %all-gather.9.cloned.1.call-start = ((), (), s32[]{:S(2)}) async-start(), calls=%async_computation.5 | async-start | bytes 2621440 | tf_op jit(solution)/shard_map/all_gather | solution.py:49
  819.0 295.2 %reduce-scatter.5.cloned.1.call-start = ((), (), s32[]{:S(2)}) async-start(), calls=%async_computation.7 | async-start | bytes 4718592 | tf_op jit(solution)/shard_map/reduce_scatter | solution.py:55
  1104.4 0.7 copy-start.1
Sparse Core Ops, SparseCore 0:
  8.9 12.4 all-gather.4
  23.3 648.2 all-gather.6
  702.9 110.7 reduce-scatter.2
  815.4 228.2 all-gather.10
  1045.1 45.9 all-gather.8
  1104.5 9.5 reduce-scatter.4
where the time goes:
time: 1120 us
  waiting for transfers between devices  1060 us (95%)
  matrix products  47.3 us (4%)
  between operations  14.2 us (1%)
    all_gather x1, waiting for transfers between devices, shards(): w_block = lax.all_gather(w_qkv, 'tok', axis=0, tiled=True)  650 us
    all_gather x1, waiting for transfers between devices, shards(): lax.all_gather(w_out, 'tok', axis=0, tiled=True)  225 us
    reduce_scatter x1, waiting for transfers between devices, shards(): lax.psum_scatter(partial_value.astype(jnp.bfloat16), 'ka', scatter_dimens...  109 us
    all_gather x1, waiting for transfers between devices, shards(): head_group = lax.all_gather(context, 'ka', axis=1, tiled=True)  47.4 us
    dot_general x1, matrix products, shards(): partial_value = jnp.dot(panel, w_block, preferred_element_type=jnp.float32)  31.1 us
  transfers between devices with their start and end apart: 6, of which 6 were waited for; matrix products, arithmetic and copies ran while one was open for 0% of the time, Pallas kernels for 0%

commit v1 on v0

--- a/solution.py
+++ b/solution.py
@@ -46,7 +46,14 @@
         "phst,pthd->pshd", prob_rows, table[:, :, :, 2], preferred_element_type=jnp.float32
     )
     context = context.astype(jnp.bfloat16).reshape(row_count, heads_dev * HD)
-    head_group = lax.all_gather(context, "ka", axis=1, tiled=True)
+    peers = lax.axis_size("ka")
+    right = [(i, (i + 1) % peers) for i in range(peers)]
+    parts = [context]
+    for far in range(1, peers):
+        parts = [lax.ppermute(parts[0], "ka", right), *parts]
+    full = jnp.concatenate(parts, axis=1)
+    shift = (lax.axis_index("ka") + 1) * parts[-1].shape[1]
+    head_group = jnp.roll(full, shift, axis=1)
     terms = jnp.dot(
         head_group,
         lax.all_gather(w_out, "tok", axis=0, tiled=True),

time: 1120 us -> 1080 us (0.964)
  waiting for transfers between devices: 1060 us -> 1000 us
    all_gather x1, waiting for transfers between devices: 225 us -> 175 us  [shards(): lax.all_gather(w_out, 'tok', axis=0, tiled=True)]
    all_gather x1 -> x0, waiting for transfers between devices: 47.4 us -> none  [shards(): head_group = lax.all_gather(context, 'ka', axis=1, tiled=True)]
    ppermute x0 -> x3, waiting for transfers between devices: none -> 42.4 us  [shards(): parts = [lax.ppermute(parts[0], 'ka', right), *parts]]
  transfers between devices with their start and end apart: 6 -> 8, of which waited for: 6 -> 8; matrix products, arithmetic and copies ran while one was open for 0% -> 1% of each run, Pallas kernels for 0% -> 0%
where the time goes in v1:
time: 1080 us
  waiting for transfers between devices  1000 us (93%)
  matrix products  46.5 us (4%)
  between operations  13.8 us (1%)
    all_gather x1, waiting for transfers between devices, shards(): w_block = lax.all_gather(w_qkv, 'tok', axis=0, tiled=True)  650 us
    all_gather x1, waiting for transfers between devices, shards(): lax.all_gather(w_out, 'tok', axis=0, tiled=True)  175 us
    reduce_scatter x1, waiting for transfers between devices, shards(): lax.psum_scatter(partial_value.astype(jnp.bfloat16), 'ka', scatter_dimens...  109 us
    ppermute x3, waiting for transfers between devices, shards(): parts = [lax.ppermute(parts[0], 'ka', right), *parts]  42.4 us
    dot_general x1, matrix products, shards(): partial_value = jnp.dot(panel, w_block, preferred_element_type=jnp.float32)  31.1 us
  transfers between devices with their start and end apart: 8, of which 8 were waited for; matrix products, arithmetic and copies ran while one was open for 1% of the time, Pallas kernels for 0%

profile of v1, /device:TPU:0, one launch (start us, length us, event | category | flops | bytes accessed | tf_op | source)
XLA Modules:
  0.0 1077.4 jit_solution(6226893992701199469)
XLA Ops:
  6.5 0.0 all-gather.4.cloned.1.call-start
  6.5 0.7 all-gather.4.cloned.1.call-update
  7.3 0.0 all-gather.6.cloned.1.call-start
  7.3 0.7 all-gather.6.cloned.1.call-update
  8.0 0.0 reduce-scatter.3.cloned.1.call-start
  8.1 13.4 %all-gather.4.cloned.1.call-done = bf16[256,3072]{1,0:T(8,128)(2,1)} async-done(((bf16[256,1536]{1,0:T(8,128)(2,1)}), bf16[256,3072]{1,0:T(8,128)(2,1)}) %all-gather.4.cloned.1.call-update) | async-done | bytes 1572880 | tf_op jit(solution)/shard_map/all_gather | solution.py:22
  21.4 650.2 %all-gather.6.cloned.1.call-done = bf16[3072,12288]{1,0:T(8,128)(2,1)} async-done(((bf16[768,12288]{1,0:T(8,128)(2,1)}), bf16[3072,12288]{1,0:T(8,128)(2,1)}) %all-gather.6.cloned.1.call-update) | async-done | bytes 75497488 | tf_op jit(solution)/shard_map/all_gather | solution.py:23
  671.6 31.1 %convolution_convert_fusion = bf16[256,12288]{1,0:T(8,128)(2,1)} fusion(bf16[256,3072]{1,0:T(8,128)(2,1)} %all-gather.4.cloned.1.call-done, bf16[3072,12288]{1,0:T(8,128)(2,1)} %all-gather.6.cloned.1.call-done), kind=kOutput, calls=%fused_computation.1 | convolution fusion | flops 19330498560 | bytes 83361792 | tf_op jit(solution)/shard_map/dot_general | solution.py:24
  702.7 0.0 reduce-scatter.3.cloned.1.call-update
  702.8 0.0 copy-start
  702.8 0.0 all-gather.8.cloned.1.call-start
  702.8 0.5 all-gather.8.cloned.1.call-update
  703.4 0.0 reduce-scatter.5.cloned.1.call-start
  703.4 0.1 copy-done
  704.1 0.1 fusion.8
  704.2 109.4 %reduce-scatter.3.cloned.1.call-done = bf16[256,3072]{1,0:T(8,128)(2,1)} async-done(((bf16[256,12288]{1,0:T(8,128)(2,1)}), bf16[256,3072]{1,0:T(8,128)(2,1)}) %reduce-scatter.3.cloned.1.call-update) | async-done | bytes 1572880 | tf_op jit(solution)/shard_map/reduce_scatter | solution.py:25
  813.7 1.7 add_convert_fusion
  815.4 0.7 copy.11
  816.1 0.9 fusion.17
  817.0 1.2 convolution_convert_fusion.1
  818.2 1.5 collective-permute-start
  819.7 14.0 %collective-permute-done = bf16[256,1024]{0,1:T(8,128)(2,1)S(1)} collective-permute-done((bf16[256,1024]{0,1:T(8,128)(2,1)S(1)}, bf16[256,1024]{0,1:T(8,128)(2,1)S(1)}, u32[]{:S(2)}, u32[]{:S(2)}) %collective-permute-start) | collective-permute-done | bytes 524320 | tf_op jit(solution)/shard_map/ppermute | solution.py:53
  833.7 0.0 collective-permute-start.1
  833.7 14.6 %collective-permute-done.1 = bf16[256,1024]{0,1:T(8,128)(2,1)S(1)} collective-permute-done((bf16[256,1024]{0,1:T(8,128)(2,1)S(1)}, bf16[256,1024]{0,1:T(8,128)(2,1)S(1)}, u32[]{:S(2)}, u32[]{:S(2)}) %collective-permute-start.1) | collective-permute-done | bytes 524320 | tf_op jit(solution)/shard_map/ppermute | solution.py:53
  848.4 0.0 collective-permute-start.2
  848.4 13.7 %collective-permute-done.2 = bf16[256,1024]{0,1:T(8,128)(2,1)S(1)} collective-permute-done((bf16[256,1024]{0,1:T(8,128)(2,1)S(1)}, bf16[256,1024]{0,1:T(8,128)(2,1)S(1)}, u32[]{:S(2)}, u32[]{:S(2)}) %collective-permute-start.2) | collective-permute-done | bytes 524320 | tf_op jit(solution)/shard_map/ppermute | solution.py:53
  862.1 0.9 constant_dynamic-update-slice_fusion.7
  863.0 0.9 constant_dynamic-update-slice_fusion.6
  863.9 0.8 constant_dynamic-update-slice_fusion.5
  864.7 0.8 constant_dynamic-update-slice_fusion.4
  865.5 0.9 constant_dynamic-update-slice_fusion.3
  866.3 0.8 constant_dynamic-update-slice_fusion.2
  867.2 0.8 constant_dynamic-update-slice_fusion.1
  868.0 0.8 constant_dynamic-update-slice_fusion
  868.8 174.9 %all-gather.8.cloned.1.call-done = bf16[4096,3072]{1,0:T(8,128)(2,1)} async-done(((bf16[1024,3072]{1,0:T(8,128)(2,1)}), bf16[4096,3072]{1,0:T(8,128)(2,1)}) %all-gather.8.cloned.1.call-update) | async-done | bytes 25165840 | tf_op jit(solution)/shard_map/all_gather | solution.py:59
  1043.7 13.3 %fusion.1 = f32[256,3072]{1,0:T(8,128)} fusion(bf16[4096,3072]{1,0:T(8,128)(2,1)} %all-gather.8.cloned.1.call-done, bf16[256,8192]{0,1:T(8,128)(2,1)} %constant_dynamic-update-slice_fusion, s32[]{:T(128)S(6)} %select_n.20), kind=kOutput, calls=%fused_computation.3 | convolution fusion | flops 6442450944 | bytes 30408708 | tf_op jit(solution)/shard_map/dot_general | solution.py:57
  1057.0 0.0 copy-start.1
  1057.0 0.0 reduce-scatter.5.cloned.1.call-update
  1057.0 0.7 copy-done.1
  1057.7 10.4 reduce-scatter.5.cloned.1.call-done
  1068.1 2.7 broadcast_add_fusion
  (3 shorter events, 0.0 us)
Async XLA Ops:
  6.5 14.9 %all-gather.4.cloned.1.call-start = ((), (), s32[]{:S(2)}) async-start(), calls=%async_computation.2 | async-start | bytes 2359296 | tf_op jit(solution)/shard_map/all_gather | solution.py:22
  7.3 664.4 %all-gather.6.cloned.1.call-start = ((), (), s32[]{:S(2)}) async-start(), calls=%async_computation.3 | async-start | bytes 94371840 | tf_op jit(solution)/shard_map/all_gather | solution.py:23
  8.0 805.7 %reduce-scatter.3.cloned.1.call-start = ((), (), s32[]{:S(2)}) async-start(), calls=%async_computation.4 | async-start | bytes 7864320 | tf_op jit(solution)/shard_map/reduce_scatter | solution.py:25
  702.8 0.7 copy-start
  702.8 340.9 %all-gather.8.cloned.1.call-start = ((), (), s32[]{:S(2)}) async-start(), calls=%async_computation.5 | async-start | bytes 31457280 | tf_op jit(solution)/shard_map/all_gather | solution.py:59
  703.4 364.7 %reduce-scatter.5.cloned.1.call-start = ((), (), s32[]{:S(2)}) async-start(), calls=%async_computation.6 | async-start | bytes 4718592 | tf_op jit(solution)/shard_map/reduce_scatter | solution.py:62
  818.2 15.6 %collective-permute-start = (bf16[256,1024]{0,1:T(8,128)(2,1)S(1)}, bf16[256,1024]{0,1:T(8,128)(2,1)S(1)}, u32[]{:S(2)}, u32[]{:S(2)}) collective-permute-start(bf16[256,1024]{0,1:T(8,128)(2,1)S(1)} %bitcast.48), channel_id=1, source_target_pairs={{0,2},{2,4},{4,6},{6,0},{1,3},{3,5},{5,7},{7,1},{8,10},{10,12},{12... | collective-permute-start | bytes 1572872 | tf_op jit(solution)/shard_map/ppermute | solution.py:53
  833.7 14.7 %collective-permute-start.1 = (bf16[256,1024]{0,1:T(8,128)(2,1)S(1)}, bf16[256,1024]{0,1:T(8,128)(2,1)S(1)}, u32[]{:S(2)}, u32[]{:S(2)}) collective-permute-start(bf16[256,1024]{0,1:T(8,128)(2,1)S(1)} %collective-permute-done), channel_id=1, source_target_pairs={{0,2},{2,4},{4,6},{6,0},{1,3},{3,5},{5,7},{7,1},{8,10},{10,12},{12... | collective-permute-start | bytes 1572872 | tf_op jit(solution)/shard_map/ppermute | solution.py:53
  848.4 13.7 %collective-permute-start.2 = (bf16[256,1024]{0,1:T(8,128)(2,1)S(1)}, bf16[256,1024]{0,1:T(8,128)(2,1)S(1)}, u32[]{:S(2)}, u32[]{:S(2)}) collective-permute-start(bf16[256,1024]{0,1:T(8,128)(2,1)S(1)} %collective-permute-done.1), channel_id=1, source_target_pairs={{0,2},{2,4},{4,6},{6,0},{1,3},{3,5},{5,7},{7,1},{8,10},{10,12},{12... | collective-permute-start | bytes 1572872 | tf_op jit(solution)/shard_map/ppermute | solution.py:53
  1057.0 0.7 copy-start.1
Sparse Core Ops, SparseCore 0:
  8.9 12.4 all-gather.3
  23.3 648.2 all-gather.5
  702.9 110.7 reduce-scatter.2
  815.4 228.2 all-gather.7
  1057.1 10.8 reduce-scatter.4
